TPU v7x, 512 devices: a whole 4x8x8 slice. The times are simulated.
512 devices in a mesh: dp: 64 (over z, y_hi, core), mp: 8 (over x, y_lo).
Axes of the slice: x: 4, y: 8 (y_hi: 4, y_lo: 2; y = y_hi * 2 + y_lo), z: 8, core: 2. Of those that a mesh axis runs over, the one named last changes fastest.
Arguments:
- queries: bfloat16 [32768, 8192], P('dp', 'mp'), may hold values from -45 to 45
- key_rows: bfloat16 [32768, 1024], P('dp', 'mp'), may hold values from -4 to 4
- value_rows: bfloat16 [32768, 1024], P('dp', 'mp'), may hold values from -6 to 6
- landmark_index: int32 [512], P('dp'), may hold values from 0 to 32767, as said below
- radius_in: float32 [512], replicated, may hold values from 0.5 to 4
- radius_out: float32 [512], replicated, may hold values from 0.02 to 0.5
Outputs:
- cross_covariance: float32 [512, 512], P('mp', 'dp')
Inputs may be any that keep to these rules, and one draw needn't show every extreme that they name: `landmark_index`: the 8 landmarks held by index d of dp name distinct tokens of sequence d, that is, positions d * 512 to (d + 1) * 512 - 1.
All inputs are finite; a program needn't handle non-finite values.
Results may differ from a plain program's by a relative error of at most 0.003.
Values may be sent and summed in bfloat16 or wider, within the bound.
No kernel may reach another device: no remote copies, remote signals or barrier semaphores. Data moves between devices by JAX's collectives and lax.ppermute only.
A program may use at most 64 MiB of HBM per device.

v0:
```python
import functools
import math
import jax
import jax.numpy as jnp
from jax import lax
from jax.sharding import PartitionSpec as P

D = 8192
HEAD_DIM = 128
EPSILON = 1e-06


def attend_head(queries, key_rows, value_rows, group_size, head_index):
    query_head = lax.dynamic_slice_in_dim(queries, head_index * HEAD_DIM, HEAD_DIM, 1)
    scores = lax.dot_general(
        query_head, key_rows, (((1,), (1,)), ((), ())), preferred_element_type=jnp.float32
    ) / math.sqrt(HEAD_DIM)
    length = queries.shape[0]
    row_position = lax.broadcasted_iota(jnp.int32, (length, length), 0)
    column_position = lax.broadcasted_iota(jnp.int32, (length, length), 1)
    scores = jnp.where(column_position <= row_position, scores, -jnp.inf)
    weights = jax.nn.softmax(scores, axis=-1).astype(jnp.bfloat16)
    return jnp.dot(weights, value_rows, preferred_element_type=jnp.float32).astype(jnp.bfloat16)


def squares_by_row(matrix):
    return jnp.sum(jnp.square(matrix.astype(jnp.float32)), axis=-1)


def inner_rows(left, right):
    return lax.dot_general(
        left, right, (((1,), (1,)), ((), ())), preferred_element_type=jnp.float32
    )


def inner_columns(left, right):
    return lax.dot_general(
        left, right, (((0,), (0,)), ((), ())), preferred_element_type=jnp.float32
    )


def center(features, totals, token_count):
    return (features.astype(jnp.float32) - totals / token_count).astype(jnp.bfloat16)


def shards(queries, key_rows, value_rows, landmark_index, radius_in, radius_out):
    length = queries.shape[0]
    heads_local = queries.shape[1] // HEAD_DIM
    group_size = heads_local // (key_rows.shape[1] // HEAD_DIM)
    per_head = lax.map(
        functools.partial(attend_head, queries, key_rows, value_rows, group_size),
        jnp.arange(heads_local, dtype=jnp.int32),
    )
    attended = jnp.transpose(per_head, (1, 0, 2)).reshape(length, heads_local * HEAD_DIM)
    landmarks = radius_in.shape[0]
    model_index = lax.axis_index("mp")
    data_index = lax.axis_index("dp")
    row_share = landmarks // lax.axis_size("mp")
    column_share = landmarks // lax.axis_size("dp")
    token_count = length * lax.axis_size("dp")
    widths = jnp.stack([radius_in, radius_out])
    own_rows = landmark_index % length
    landmark_rows = jnp.stack(
        [jnp.take(queries, own_rows, axis=0), jnp.take(attended, own_rows, axis=0)]
    )
    row_norms = jnp.stack([squares_by_row(queries), squares_by_row(attended)])
    landmark_piece = lax.all_gather(landmark_rows, "dp", axis=1, tiled=True)
    mark_norms = squares_by_row(landmark_piece)
    cross = jnp.stack(
        [inner_rows(queries, landmark_piece[0]), inner_rows(attended, landmark_piece[1])]
    )
    distance_part = row_norms[:, :, None] + mark_norms[:, None, :] - 2.0 * cross
    distance = lax.psum(distance_part, "mp")
    features = jnp.exp(-distance / (D * widths[:, None, :])).astype(jnp.bfloat16)
    row_features = lax.dynamic_slice_in_dim(features[0], model_index * row_share, row_share, 1)
    column_features = features[1]
    row_total, column_total = lax.psum(
        (
            jnp.sum(row_features.astype(jnp.float32), axis=0),
            jnp.sum(column_features.astype(jnp.float32), axis=0),
        ),
        "dp",
    )
    rows_centered = center(row_features, row_total[None, :], token_count)
    columns_centered = center(column_features, column_total[None, :], token_count)
    second = inner_columns(rows_centered, columns_centered)
    row_spread = jnp.sum(jnp.square(rows_centered.astype(jnp.float32)), axis=0)
    column_spread = jnp.sum(jnp.square(columns_centered.astype(jnp.float32)), axis=0)
    second, row_spread, column_spread = lax.psum((second, row_spread, column_spread), "dp")
    own_block = lax.dynamic_slice_in_dim(second, data_index * column_share, column_share, 1)
    column_spread = lax.dynamic_slice_in_dim(
        column_spread, data_index * column_share, column_share, 0
    )
    covariance = own_block / token_count
    spread_rows = row_spread / token_count
    spread_columns = column_spread / token_count
    return covariance / jnp.sqrt(
        (spread_rows + EPSILON)[:, None] * (spread_columns + EPSILON)[None, :]
    )


def solution(mesh):
    return jax.shard_map(
        shards,
        mesh=mesh,
        in_specs=(P("dp", "mp"), P("dp", "mp"), P("dp", "mp"), P("dp"), P(), P()),
        out_specs=P("mp", "dp"),
        check_vma=False,
    )
```

profile of v0, /device:TPU:1, one launch (start us, length us, event | category | flops | bytes accessed | tf_op | source)
XLA Modules:
  0.0 903.9 jit_solution(17541337728010904406)
XLA Ops:
  6.5 0.7 compare_and_fusion
  7.2 1.9 gather_fusion
  9.2 26.6 %while.10 = (s32[]{:T(128)}, bf16[8,512,128]{2,1,0:T(8,128)(2,1)S(1)}, s32[8]{0:T(128)S(1)}, bf16[512,1024]{1,0:T(8,128)(2,1)}, bf16[512,128]{1,0:T(8,128)(2,1)}...) while((s32[]{:T(128)}, bf16[8,512,128]{2,1,0:T(8,128)(2,1)S(1)}, ...), condition=%wide.region_4.5_spmd, body=%wide.region_1.4_spmd.sunk | while | flops 136641536 | bytes 4204747 | solution.py:50
  9.2 0.7 dynamic_slice.34
  10.6 1.3 fusion.39
  11.9 0.2 fusion.40
  12.1 0.4 fusion.41
  12.5 0.7 dynamic_slice.34
  13.9 1.3 fusion.39
  15.2 0.2 fusion.40
  15.4 0.4 fusion.41
  15.9 0.7 dynamic_slice.34
  17.2 1.3 fusion.39
  18.5 0.2 fusion.40
  18.7 0.4 fusion.41
  19.2 0.7 dynamic_slice.34
  20.5 1.3 fusion.39
  21.8 0.2 fusion.40
  22.0 0.4 fusion.41
  22.5 0.7 dynamic_slice.34
  23.9 1.3 fusion.39
  25.2 0.2 fusion.40
  25.4 0.4 fusion.41
  25.8 0.7 dynamic_slice.34
  27.2 1.3 fusion.39
  28.5 0.2 fusion.40
  28.7 0.4 fusion.41
  29.2 0.7 dynamic_slice.34
  30.5 1.3 fusion.39
  31.8 0.2 fusion.40
  32.0 0.4 fusion.41
  32.5 0.7 dynamic_slice.34
  33.9 1.3 fusion.39
  35.1 0.2 fusion.40
  35.3 0.4 fusion.41
  35.8 0.1 copy_bitcast_fusion
  36.0 0.6 gather_fusion.1
  36.5 0.1 select_bitcast_fusion.1
  36.6 0.6 pad_maximum_fusion
  37.2 0.0 all-gather.2.cloned.1.call-update
  37.2 0.0 all-reduce.5.cloned.1.call-start
  37.3 0.3 multiply_reduce_fusion.2
  37.6 0.3 multiply_reduce_fusion.1
  37.9 89.6 %all-gather.2.cloned.1.call-done = bf16[2,512,1024]{2,1,0:T(8,128)(2,1)} async-done(((bf16[2,8,1024]{2,1,0:T(8,128)(2,1)}), bf16[2,512,1024]{2,1,0:T(8,128)(2,1)}) %all-gather.2.cloned.1.call-update) | async-done | bytes 2097168 | tf_op jit(solution)/shard_map/all_gather | solution.py:67
  127.4 2.1 convolution_bitcast_fusion
  129.6 0.5 multiply_reduce_fusion
  130.1 0.8 convolution_bitcast_fusion.1
  130.8 1.6 fusion.8
  132.4 0.0 all-reduce.5.cloned.1.call-update
  132.4 0.0 all-reduce.7.cloned.1.call-start
  132.5 0.6 copy-done.2
  133.1 110.2 %all-reduce.5.cloned.1.call-done = f32[2,512,512]{1,2,0:T(8,128)} async-done(((f32[2,512,512]{1,2,0:T(8,128)}), f32[2,512,512]{1,2,0:T(8,128)}) %all-reduce.5.cloned.1.call-update) | async-done | bytes 2097168 | tf_op jit(solution)/shard_map/psum | solution.py:73
  243.3 2.0 exponential_convert_fusion
  245.4 0.1 convert_reduce_fusion
  245.6 0.1 convert_reduce_fusion.1
  245.7 139.0 %all-reduce.1 = (f32[512]{0:T(512)S(1)}, f32[64]{0:T(128)S(1)}) all-reduce(f32[512]{0:T(512)S(1)} %convert_reduce_fusion, f32[64]{0:T(128)S(1)} %convert_reduce_fusion.1), channel_id=1, replica_groups=mesh['dp'=64,'mp'=8] {'dp'}, use_global_device_ids=true, to_apply=%region_11.13 | all-reduce | flops 576 | bytes 4608 | tf_op jit(solution)/shard_map/psum | solution.py:77
  384.7 0.2 multiply_reduce_fusion.4
  384.9 1.1 fusion.13
  386.0 0.3 multiply_reduce_fusion.3
  386.3 0.0 all-reduce.7.cloned.1.call-update
  386.3 143.5 %all-reduce = (f32[512]{0:T(512)S(1)}, f32[64]{0:T(128)S(1)}) all-reduce(f32[512]{0:T(512)S(1)} %multiply_reduce_fusion.3, f32[64]{0:T(128)S(1)} %multiply_reduce_fusion.4), channel_id=1, replica_groups=mesh['dp'=64,'mp'=8] {'dp'}, use_global_device_ids=true, to_apply=%region_16.18 | all-reduce | flops 576 | bytes 4608 | tf_op jit(solution)/shard_map/psum | solution.py:89
  529.9 0.1 multiply_add_fusion
  529.9 366.1 %all-reduce.7.cloned.1.call-done = f32[64,512]{0,1:T(8,128)} async-done(((f32[64,512]{0,1:T(8,128)}), f32[64,512]{0,1:T(8,128)}) %all-reduce.7.cloned.1.call-update) | async-done | bytes 131088 | tf_op jit(solution)/shard_map/psum | solution.py:89
  896.0 1.3 rsqrt_multiply_fusion
  (33 shorter events, 0.2 us)
Async XLA Ops:
  6.5 120.9 %all-gather.2.cloned.1.call-start = ((), (), s32[]{:S(2)}) async-start(), calls=%async_computation | async-start | bytes 2129920 | tf_op jit(solution)/shard_map/all_gather | solution.py:67
  9.2 2.9 copy-start.4
  12.5 2.9 copy-start.4
  15.8 2.9 copy-start.4
  19.2 2.9 copy-start.4
  22.5 2.9 copy-start.4
  25.8 2.9 copy-start.4
  29.1 2.9 copy-start.4
  32.5 2.9 copy-start.4
  35.8 1.5 copy-start.1
  37.2 206.1 %all-reduce.5.cloned.1.call-start = ((), (), s32[]{:S(2)}) async-start(), calls=%async_computation.1 | async-start | bytes 4194304 | tf_op jit(solution)/shard_map/psum | solution.py:73
  127.4 2.1 copy-start
  132.4 0.7 copy-start.2
  132.4 0.7 copy-start.3
  132.4 763.6 %all-reduce.7.cloned.1.call-start = ((), (), s32[]{:S(2)}) async-start(), calls=%async_computation.2 | async-start | bytes 524288 | tf_op jit(solution)/shard_map/psum | solution.py:89
Sparse Core Ops, SparseCore 0:
  37.4 90.0 all-gather.1
  132.6 110.7 all-reduce.4
  386.4 509.5 all-reduce.6
where the time goes:
time: 904 us
  waiting for transfers between devices  566 us (63%)
  blocking collectives  283 us (31%)
  matrix products  17.8 us (2%)
  between operations  13.2 us (1%)
  other arithmetic  9.8 us (1%)
    psum x1, waiting for transfers between devices, shards(): lax.psum((second, row_spread, column_spread), 'dp')  366 us
    psum x1, blocking collectives, shards(): lax.psum((second, row_spread, column_spread), 'dp')  144 us
    psum x1, blocking collectives, shards(): lax.psum((jnp.sum(row_features.astype(jnp.float32), axis=0), jnp.sum(colu...  139 us
    psum x1, waiting for transfers between devices, shards(): distance = lax.psum(distance_part, 'mp')  110 us
    all_gather x1, waiting for transfers between devices, shards(): landmark_piece = lax.all_gather(landmark_rows, 'dp', axis=1, tiled=True)  89.6 us
  transfers between devices with their start and end apart: 3, of which 3 were waited for; matrix products, arithmetic and copies ran while one was open for 0% of the time, Pallas kernels for 0%

commit v1 on v0

--- a/solution.py
+++ b/solution.py
@@ -8,6 +8,11 @@
 D = 8192
 HEAD_DIM = 128
 EPSILON = 1e-06
+
+
+def add_all(x, name):
+    shards = lax.all_gather(x, name)
+    return jnp.sum(shards, axis=0)
 
 
 def attend_head(queries, key_rows, value_rows, group_size, head_index):
@@ -70,7 +75,7 @@
         [inner_rows(queries, landmark_piece[0]), inner_rows(attended, landmark_piece[1])]
     )
     distance_part = row_norms[:, :, None] + mark_norms[:, None, :] - 2.0 * cross
-    distance = lax.psum(distance_part, "mp")
+    distance = add_all(distance_part, "mp")
     features = jnp.exp(-distance / (D * widths[:, None, :])).astype(jnp.bfloat16)
     row_features = lax.dynamic_slice_in_dim(features[0], model_index * row_share, row_share, 1)
     column_features = features[1]

time: 904 us -> 1130 us (1.25)
  waiting for transfers between devices: 566 us -> 783 us
    all_gather x0 -> x1, waiting for transfers between devices: none -> 326 us  [add_all(): shards = lax.all_gather(x, name)]
    psum x1 -> x0, waiting for transfers between devices: 110 us -> none  [shards(): distance = lax.psum(distance_part, 'mp')]
where the time goes in v1:
time: 1130 us
  waiting for transfers between devices  783 us (69%)
  blocking collectives  283 us (25%)
  matrix products  17.7 us (2%)
  other arithmetic  15.7 us (1%)
  between operations  13.2 us (1%)
  local copies, waits for them, and re-layouts  12.2 us (1%)
    psum x1, waiting for transfers between devices, shards(): lax.psum((second, row_spread, column_spread), 'dp')  367 us
    all_gather x1, waiting for transfers between devices, add_all(): shards = lax.all_gather(x, name)  326 us
    psum x1, blocking collectives, shards(): lax.psum((second, row_spread, column_spread), 'dp')  144 us
    psum x1, blocking collectives, shards(): lax.psum((jnp.sum(row_features.astype(jnp.float32), axis=0), jnp.sum(colu...  139 us
    all_gather x1, waiting for transfers between devices, shards(): landmark_piece = lax.all_gather(landmark_rows, 'dp', axis=1, tiled=True)  89.6 us
  transfers between devices with their start and end apart: 3, of which 3 were waited for; matrix products, arithmetic and copies ran while one was open for 0% of the time, Pallas kernels for 0%

profile of v1, /device:TPU:1, one launch (start us, length us, event | category | flops | bytes accessed | tf_op | source)
XLA Modules:
  0.0 1130.0 jit_solution(17074158252670107869)
XLA Ops:
  6.5 26.5 %while.10 = (s32[]{:T(128)}, bf16[8,512,128]{2,1,0:T(8,128)(2,1)S(1)}, s32[8]{0:T(128)S(1)}, bf16[512,1024]{1,0:T(8,128)(2,1)}, bf16[512,128]{1,0:T(8,128)(2,1)}...) while((s32[]{:T(128)}, bf16[8,512,128]{2,1,0:T(8,128)(2,1)S(1)}, ...), condition=%wide.region_4.5_spmd, body=%wide.region_1.4_spmd.sunk | while | flops 136641536 | bytes 4204739 | solution.py:55
  6.5 0.7 dynamic_slice.34
  7.9 1.3 fusion.39
  9.2 0.2 fusion.40
  9.4 0.4 fusion.41
  9.9 0.7 dynamic_slice.34
  11.2 1.3 fusion.39
  12.5 0.2 fusion.40
  12.7 0.4 fusion.41
  13.2 0.7 dynamic_slice.34
  14.5 1.3 fusion.39
  15.8 0.2 fusion.40
  16.0 0.4 fusion.41
  16.5 0.7 dynamic_slice.34
  17.9 1.3 fusion.39
  19.2 0.2 fusion.40
  19.4 0.4 fusion.41
  19.8 0.7 dynamic_slice.34
  21.2 1.3 fusion.39
  22.5 0.2 fusion.40
  22.7 0.4 fusion.41
  23.1 0.7 dynamic_slice.34
  24.5 1.3 fusion.39
  25.8 0.2 fusion.40
  26.0 0.4 fusion.41
  26.4 0.7 dynamic_slice.34
  27.8 1.3 fusion.39
  29.1 0.2 fusion.40
  29.3 0.4 fusion.41
  29.8 0.7 dynamic_slice.34
  31.1 1.3 fusion.39
  32.4 0.2 fusion.40
  32.6 0.4 fusion.41
  33.1 0.1 copy_bitcast_fusion
  33.2 0.5 copy-done.5
  33.8 0.6 copy-done.1
  34.3 0.6 gather_fusion
  34.9 0.6 gather_fusion.1
  35.5 0.1 select_bitcast_fusion.1
  35.5 0.6 pad_maximum_fusion
  36.2 0.0 all-gather.5.cloned.1.call-start
  36.2 0.3 multiply_reduce_fusion.1
  36.5 0.3 multiply_reduce_fusion.2
  36.8 89.6 %all-gather.3.cloned.1.call-done = bf16[2,512,1024]{2,1,0:T(8,128)(2,1)} async-done(((bf16[2,8,1024]{2,1,0:T(8,128)(2,1)}), bf16[2,512,1024]{2,1,0:T(8,128)(2,1)}) %all-gather.3.cloned.1.call-update) | async-done | bytes 2097168 | tf_op jit(solution)/shard_map/all_gather | solution.py:72
  126.4 2.1 convolution_bitcast_fusion
  128.5 0.7 convolution_bitcast_fusion.1
  129.2 0.5 multiply_reduce_fusion
  129.7 0.3 fusion.8
  130.0 1.9 copy.11
  132.0 0.6 copy-done.2
  132.6 326.1 %all-gather.5.cloned.1.call-done = f32[8,2,512,512]{3,2,1,0:T(8,128)} async-done(((f32[1,2,512,512]{3,2,1,0:T(8,128)}), f32[8,2,512,512]{3,2,1,0:T(8,128)}) %all-gather.5.cloned.1.call-update) | async-done | bytes 16777232 | tf_op jit(solution)/shard_map/all_gather | solution.py:14
  458.7 9.4 reduce_sum.84
  468.2 1.9 copy.14
  470.1 0.4 exponential_convert_fusion
  470.6 0.1 convert_reduce_fusion
  470.7 0.1 convert_reduce_fusion.1
  470.8 138.8 %all-reduce.1 = (f32[512]{0:T(512)S(1)}, f32[64]{0:T(128)S(1)}) all-reduce(f32[512]{0:T(512)S(1)} %convert_reduce_fusion, f32[64]{0:T(128)S(1)} %convert_reduce_fusion.1), channel_id=1, replica_groups=mesh['dp'=64,'mp'=8] {'dp'}, use_global_device_ids=true, to_apply=%region_11.13 | all-reduce | flops 576 | bytes 4608 | tf_op jit(solution)/shard_map/psum | solution.py:82
  609.7 0.2 multiply_reduce_fusion.4
  609.9 0.3 multiply_reduce_fusion.3
  610.2 1.1 fusion.13
  611.3 143.7 %all-reduce = (f32[512]{0:T(512)S(1)}, f32[64]{0:T(128)S(1)}) all-reduce(f32[512]{0:T(512)S(1)} %multiply_reduce_fusion.3, f32[64]{0:T(128)S(1)} %multiply_reduce_fusion.4), channel_id=1, replica_groups=mesh['dp'=64,'mp'=8] {'dp'}, use_global_device_ids=true, to_apply=%region_16.18 | all-reduce | flops 576 | bytes 4608 | tf_op jit(solution)/shard_map/psum | solution.py:94
  755.0 0.1 multiply_add_fusion
  755.1 367.0 %all-reduce.4.cloned.1.call-done = f32[64,512]{0,1:T(8,128)} async-done(((f32[64,512]{0,1:T(8,128)}), f32[64,512]{0,1:T(8,128)}) %all-reduce.4.cloned.1.call-update) | async-done | bytes 131088 | tf_op jit(solution)/shard_map/psum | solution.py:94
  1122.1 1.3 rsqrt_multiply_fusion
  (38 shorter events, 0.3 us)
Async XLA Ops:
  6.5 119.8 %all-gather.3.cloned.1.call-start = ((), (), s32[]{:S(2)}) async-start(), calls=%async_computation | async-start | bytes 2129920 | tf_op jit(solution)/shard_map/all_gather | solution.py:72
  6.5 2.9 copy-start.4
  9.8 2.9 copy-start.4
  13.2 2.9 copy-start.4
  16.5 2.9 copy-start.4
  19.8 2.9 copy-start.4
  23.1 2.9 copy-start.4
  26.4 2.9 copy-start.4
  29.8 2.9 copy-start.4
  33.1 0.7 copy-start.5
  33.1 1.2 copy-start.1
  36.2 422.6 %all-gather.5.cloned.1.call-start = ((), (), s32[]{:S(2)}) async-start(), calls=%async_computation.1 | async-start | bytes 18874368 | tf_op jit(solution)/shard_map/all_gather | solution.py:14
  126.4 2.1 copy-start
  131.9 0.7 copy-start.2
  131.9 0.7 copy-start.3
  131.9 990.2 %all-reduce.4.cloned.1.call-start = ((), (), s32[]{:S(2)}) async-start(), calls=%async_computation.2 | async-start | bytes 524288 | tf_op jit(solution)/shard_map/psum | solution.py:94
Sparse Core Ops, SparseCore 0:
  36.3 90.0 all-gather.2
  132.0 326.6 all-gather.4
  611.4 510.6 all-reduce.3
